TPU v7x, 32 devices: a whole 2x2x4 slice. The times are simulated.
32 devices in a mesh: cells: 32 (over z, y, x, core).
Axes of the slice: x: 2, y: 2, z: 4, core: 2. Of those that a mesh axis runs over, the one named last changes fastest.
Arguments:
- concentration: float32 [9, 256, 4096], P(None, None, 'cells'), may hold values from 0.05 to 4
- flux_weight: float32 [8, 9, 4096], P(None, None, 'cells'), may hold values from 0.01 to 0.08
- vertical_mixing: float32 [8, 4096], P(None, 'cells'), may hold values from 0.02 to 0.15
- deposition: float32 [9, 4096], P(None, 'cells'), may hold values from 0.02 to 0.3
- halo_index: int32 [8, 4096], P(None, 'cells'), may hold values from 0 to 639, as said below
- send_cells: int32 [32, 32, 16], P('cells'), may hold values from 0 to 127, as said below
- live_count: int32 [32], P('cells'), may hold values from 32 to 128, as said below
Outputs:
- advanced: float32 [9, 256, 4096], P(None, None, 'cells')
Inputs may be any that keep to these rules, and one draw needn't show every extreme that they name: Device d's live cells are its slots 0 to live_count[d] - 1; some device is full in every draw. send_cells[d, p, h] is a live slot of device d. `halo_index`: every entry of a live cell of device d is a live slot of d below 128, or 128 + p * 16 + h for a sender p equal to d - 2, d - 1, d + 1 or d + 2 within the axis, or to (d + 16) mod 32.
All inputs are finite; a program needn't handle non-finite values.
Results may differ from a plain program's by a relative error of at most 0.00002.
Values sent between devices are 32-bit elements; how exact they have to be, the bound alone decides.
No kernel may reach another device: no remote copies, remote signals or barrier semaphores. Data moves between devices by JAX's collectives and lax.ppermute only.
A program may use at most 128 MiB of HBM per device.

v0:
```python
import jax
import jax.numpy as jnp
from jax import lax
from jax.sharding import PartitionSpec as P

STEPS = 2


def advance(values, extended, lookup, flux_weight, vertical_mixing, deposition, occupied, length):
    levels, pulses = (values.shape[0], values.shape[1])
    summed = jnp.zeros_like(values)
    for neighbour in range(flux_weight.shape[0]):
        columns = lookup[neighbour]
        nearby = jnp.take(extended, columns, axis=1).reshape(levels, pulses, length)
        weight = flux_weight[neighbour]
        summed = summed + weight[:, None, :] * (nearby - values)
    upward = vertical_mixing[:, None, :] * (values[1:] - values[:-1])
    nothing = jnp.zeros_like(values[:1])
    vertical = jnp.concatenate([upward, nothing], axis=0) - jnp.concatenate(
        [nothing, upward], axis=0
    )
    living = jnp.arange(length, dtype=jnp.int32) < occupied
    return jnp.where(
        living[None, None, :], (values + summed + vertical) * (1.0 - deposition[:, None, :]), 0.0
    )


def per_device(
    concentration, flux_weight, vertical_mixing, deposition, halo_index, send_cells, live_count
):
    levels, pulses, capacity = concentration.shape
    sender_rows = send_cells[0]
    occupied = live_count[0]
    values = concentration
    for sweep in range(STEPS):
        flat_values = values.reshape(levels * pulses, capacity)
        outgoing = jnp.take(flat_values, sender_rows.reshape(-1), axis=1)
        incoming = lax.all_to_all(outgoing, "cells", split_axis=1, concat_axis=1, tiled=True)
        extended = jnp.concatenate([flat_values, incoming], axis=1)
        values = advance(
            values,
            extended,
            halo_index,
            flux_weight,
            vertical_mixing,
            deposition,
            occupied,
            capacity,
        )
    return values


def solution(mesh):
    in_specs = (
        P(None, None, "cells"),
        P(None, None, "cells"),
        P(None, "cells"),
        P(None, "cells"),
        P(None, "cells"),
        P("cells", None, None),
        P("cells"),
    )
    out_specs = P(None, None, "cells")
    return jax.shard_map(
        per_device, mesh=mesh, in_specs=in_specs, out_specs=out_specs, check_vma=False
    )
```

profile of v0, /device:TPU:0, one launch (start us, length us, event | category | flops | bytes accessed | tf_op | source)
XLA Modules:
  0.0 380.0 jit_solution(717401835810015343)
XLA Ops:
  0.0 0.8 copy.27
  0.9 1.6 copy.29
  2.6 4.0 %gather_fusion = f32[512,2304]{1,0:T(8,128)} fusion(f32[2304,128]{0,1:T(8,128)S(1)} %copy.29, s32[1024]{0:T(1024)S(1)} %pad_clamp_fusion.8), kind=kCustom, calls=%fused_computation.clone | custom fusion | bytes 9439232 | tf_op jit(solution)/shard_map/jit(_take)/gather | solution.py:37
  6.6 4.8 %broadcast_select_fusion.1 = f32[512,2304]{1,0:T(8,128)} fusion(f32[512,2304]{1,0:T(8,128)} %gather_fusion, pred[512]{0:T(512)(128)(4,1)S(1)} %compare_and_fusion.8), kind=kLoop, calls=%fused_computation.21 | loop fusion | flops 1179648 | bytes 9437696 | tf_op jit(solution)/shard_map/jit(_take)/select_n | solution.py:37
  11.4 7.4 %all-to-all-start = ((f32[2304,32,16]{0,2,1:T(8,128)}), f32[2304,32,16]{0,2,1:T(8,128)}, u32[]{:S(2)}, u32[]{:S(2)}) async-start(f32[2304,32,16]{0,2,1:T(8,128)} %bitcast.109), calls=%async_computation | async-start | bytes 9437184 | tf_op jit(solution)/shard_map/all_to_all | solution.py:38
  18.9 0.6 copy.74
  20.7 0.6 copy.77
  23.7 0.6 compare_and_fusion.7
  26.1 0.6 pad_clamp_fusion.3
  29.7 1.1 subtract_multiply_fusion
  30.8 93.4 %all-to-all-done = f32[2304,32,16]{0,2,1:T(8,128)} async-done(((f32[2304,32,16]{0,2,1:T(8,128)}), f32[2304,32,16]{0,2,1:T(8,128)}, u32[]{:S(2)}, u32[]{:S(2)}) %all-to-all-start) | async-done | bytes 4718624 | tf_op jit(solution)/shard_map/all_to_all | solution.py:38
  124.2 5.2 %pad_maximum_fusion = f32[2304,640]{0,1:T(8,128)} fusion(f32[2304,512]{0,1:T(8,128)} %bitcast.6, f32[2304,128]{0,1:T(8,128)S(1)} %copy.29), kind=kLoop, calls=%fused_computation.18 | loop fusion | flops 1474560 | bytes 11796480 | tf_op jit(solution)/shard_map/concatenate | solution.py:39
  129.4 4.4 %gather_fusion.2 = f32[128,2304]{1,0:T(8,128)S(1)} fusion(f32[2304,640]{0,1:T(8,128)} %pad_maximum_fusion, s32[1024]{0:T(1024)} %pad_clamp_fusion.6), kind=kCustom, calls=%fused_computation.3.clone | custom fusion | bytes 2359808 | tf_op jit(solution)/shard_map/jit(_take)/gather | solution.py:14
  133.8 0.7 select_bitcast_fusion.14
  134.5 1.4 copy.32
  135.9 4.4 %gather_fusion.3 = f32[128,2304]{1,0:T(8,128)S(1)} fusion(f32[2304,640]{0,1:T(8,128)} %pad_maximum_fusion, s32[1024]{0:T(1024)} %pad_clamp_fusion.5), kind=kCustom, calls=%fused_computation.4.clone | custom fusion | bytes 2359808 | tf_op jit(solution)/shard_map/jit(_take)/gather | solution.py:14
  140.3 0.8 select_bitcast_fusion.13
  141.0 1.4 copy.34
  142.4 4.4 %gather_fusion.4 = f32[128,2304]{1,0:T(8,128)S(1)} fusion(f32[2304,640]{0,1:T(8,128)} %pad_maximum_fusion, s32[1024]{0:T(1024)} %pad_clamp_fusion.4), kind=kCustom, calls=%fused_computation.5.clone | custom fusion | bytes 2359808 | tf_op jit(solution)/shard_map/jit(_take)/gather | solution.py:14
  146.8 0.7 select_bitcast_fusion.12
  147.5 1.4 copy.36
  148.9 4.4 %gather_fusion.5 = f32[128,2304]{1,0:T(8,128)S(1)} fusion(f32[2304,640]{0,1:T(8,128)} %pad_maximum_fusion, s32[1024]{0:T(1024)} %pad_clamp_fusion.3), kind=kCustom, calls=%fused_computation.6.clone | custom fusion | bytes 2359808 | tf_op jit(solution)/shard_map/jit(_take)/gather | solution.py:14
  153.3 0.8 select_bitcast_fusion.11
  154.1 1.5 copy.38
  155.5 4.4 %gather_fusion.6 = f32[128,2304]{1,0:T(8,128)S(1)} fusion(f32[2304,640]{0,1:T(8,128)} %pad_maximum_fusion, s32[1024]{0:T(1024)} %pad_clamp_fusion.2), kind=kCustom, calls=%fused_computation.7.clone | custom fusion | bytes 2359808 | tf_op jit(solution)/shard_map/jit(_take)/gather | solution.py:14
  159.9 0.8 select_bitcast_fusion.10
  160.7 1.4 copy.40
  162.1 4.4 %gather_fusion.7 = f32[128,2304]{1,0:T(8,128)S(1)} fusion(f32[2304,640]{0,1:T(8,128)} %pad_maximum_fusion, s32[1024]{0:T(1024)} %pad_clamp_fusion.1), kind=kCustom, calls=%fused_computation.8.clone | custom fusion | bytes 2359808 | tf_op jit(solution)/shard_map/jit(_take)/gather | solution.py:14
  166.5 0.8 select_bitcast_fusion.9
  167.2 1.4 copy.42
  168.6 4.4 %gather_fusion.1 = f32[128,2304]{1,0:T(8,128)S(1)} fusion(f32[2304,640]{0,1:T(8,128)} %pad_maximum_fusion, s32[1024]{0:T(1024)} %pad_clamp_fusion.7), kind=kCustom, calls=%fused_computation.1.clone | custom fusion | bytes 2359808 | tf_op jit(solution)/shard_map/jit(_take)/gather | solution.py:14
  173.0 0.8 select_bitcast_fusion.15
  173.8 1.4 copy.30
  175.2 4.4 %gather_fusion.8 = f32[128,2304]{1,0:T(8,128)S(1)} fusion(f32[2304,640]{0,1:T(8,128)} %pad_maximum_fusion, s32[1024]{0:T(1024)} %pad_clamp_fusion), kind=kCustom, calls=%fused_computation.9.clone | custom fusion | bytes 2359808 | tf_op jit(solution)/shard_map/jit(_take)/gather | solution.py:14
  179.6 0.8 select_bitcast_fusion.8
  180.4 1.4 copy.44
  181.8 6.0 %multiply_select_fusion.1 = f32[9,256,128]{2,1,0:T(8,128)S(1)} fusion(f32[8,256,128]{2,1,0:T(8,128)} %subtract_multiply_fusion, f32[9,256,128]{2,1,0:T(8,128)S(1)} %copy-done, f32[9,256,128]{2,1,0:T(8,128)} %bitcast.127, f32[9,256,128]{2,1,0:T(8,128)} %bitcast.125, f32[9,256,128]{2,1,0:T(8,128)} %bitcast.122, f32[9,256,128]{2,1,0:T(8,128)} %bitcast.121, ...), kind=kLoop, calls=%fused_computation.39 | loop fusion | flops 8257536 | bytes 12886656 | tf_op jit(solution)/shard_map/jit(_where)/select_n | solution.py:23
  188.5 4.0 %gather_fusion.9 = f32[512,2304]{1,0:T(8,128)} fusion(f32[2304,128]{0,1:T(8,128)S(1)} %copy.46, s32[1024]{0:T(1024)S(1)} %copy-done.7), kind=kCustom, calls=%fused_computation.2.clone | custom fusion | bytes 9439232 | tf_op jit(solution)/shard_map/jit(_take)/gather | solution.py:37
  192.5 4.8 %broadcast_select_fusion = f32[512,2304]{1,0:T(8,128)} fusion(f32[512,2304]{1,0:T(8,128)} %gather_fusion.9, pred[512]{0:T(512)(128)(4,1)S(1)} %copy-done.10), kind=kLoop, calls=%fused_computation.20 | loop fusion | flops 1179648 | bytes 9437696 | tf_op jit(solution)/shard_map/jit(_take)/select_n | solution.py:37
  197.3 3.9 %all-to-all-start.1 = ((f32[2304,32,16]{0,2,1:T(8,128)}), f32[2304,32,16]{0,2,1:T(8,128)}, u32[]{:S(2)}, u32[]{:S(2)}) async-start(f32[2304,32,16]{0,2,1:T(8,128)} %bitcast.110), calls=%async_computation.1 | async-start | bytes 9437184 | tf_op jit(solution)/shard_map/all_to_all | solution.py:38
  201.2 1.1 fusion
  202.3 104.2 %all-to-all-done.1 = f32[2304,32,16]{0,2,1:T(8,128)} async-done(((f32[2304,32,16]{0,2,1:T(8,128)}), f32[2304,32,16]{0,2,1:T(8,128)}, u32[]{:S(2)}, u32[]{:S(2)}) %all-to-all-start.1) | async-done | bytes 4718624 | tf_op jit(solution)/shard_map/all_to_all | solution.py:38
  306.5 5.2 %pad_maximum_fusion.1 = f32[2304,640]{0,1:T(8,128)} fusion(f32[2304,512]{0,1:T(8,128)} %bitcast.40, f32[2304,128]{0,1:T(8,128)S(1)} %copy.46), kind=kLoop, calls=%fused_computation.19 | loop fusion | flops 1474560 | bytes 11796480 | tf_op jit(solution)/shard_map/concatenate | solution.py:39
  311.7 5.4 %gather_fusion.10 = f32[128,2304]{1,0:T(8,128)} fusion(f32[2304,640]{0,1:T(8,128)} %pad_maximum_fusion.1, s32[1024]{0:T(1024)} %pad_clamp_fusion.7), kind=kCustom, calls=%fused_computation.10.clone | custom fusion | bytes 2359808 | tf_op jit(solution)/shard_map/jit(_take)/gather | solution.py:14
  317.1 5.3 %gather_fusion.11 = f32[128,2304]{1,0:T(8,128)} fusion(f32[2304,640]{0,1:T(8,128)} %pad_maximum_fusion.1, s32[1024]{0:T(1024)} %pad_clamp_fusion.6), kind=kCustom, calls=%fused_computation.11.clone | custom fusion | bytes 2359808 | tf_op jit(solution)/shard_map/jit(_take)/gather | solution.py:14
  322.4 5.3 %gather_fusion.12 = f32[128,2304]{1,0:T(8,128)} fusion(f32[2304,640]{0,1:T(8,128)} %pad_maximum_fusion.1, s32[1024]{0:T(1024)} %pad_clamp_fusion.5), kind=kCustom, calls=%fused_computation.12.clone | custom fusion | bytes 2359808 | tf_op jit(solution)/shard_map/jit(_take)/gather | solution.py:14
  327.8 5.3 %gather_fusion.13 = f32[128,2304]{1,0:T(8,128)} fusion(f32[2304,640]{0,1:T(8,128)} %pad_maximum_fusion.1, s32[1024]{0:T(1024)} %pad_clamp_fusion.4), kind=kCustom, calls=%fused_computation.13.clone | custom fusion | bytes 2359808 | tf_op jit(solution)/shard_map/jit(_take)/gather | solution.py:14
  333.1 5.3 %gather_fusion.14 = f32[128,2304]{1,0:T(8,128)} fusion(f32[2304,640]{0,1:T(8,128)} %pad_maximum_fusion.1, s32[1024]{0:T(1024)} %pad_clamp_fusion.3), kind=kCustom, calls=%fused_computation.14.clone | custom fusion | bytes 2359808 | tf_op jit(solution)/shard_map/jit(_take)/gather | solution.py:14
  338.4 5.4 %gather_fusion.15 = f32[128,2304]{1,0:T(8,128)} fusion(f32[2304,640]{0,1:T(8,128)} %pad_maximum_fusion.1, s32[1024]{0:T(1024)} %pad_clamp_fusion.2), kind=kCustom, calls=%fused_computation.15.clone | custom fusion | bytes 2359808 | tf_op jit(solution)/shard_map/jit(_take)/gather | solution.py:14
  343.8 5.3 %gather_fusion.16 = f32[128,2304]{1,0:T(8,128)} fusion(f32[2304,640]{0,1:T(8,128)} %pad_maximum_fusion.1, s32[1024]{0:T(1024)} %pad_clamp_fusion.1), kind=kCustom, calls=%fused_computation.16.clone | custom fusion | bytes 2359808 | tf_op jit(solution)/shard_map/jit(_take)/gather | solution.py:14
  349.2 5.3 %gather_fusion.17 = f32[128,2304]{1,0:T(8,128)} fusion(f32[2304,640]{0,1:T(8,128)} %pad_maximum_fusion.1, s32[1024]{0:T(1024)} %pad_clamp_fusion), kind=kCustom, calls=%fused_computation.17.clone | custom fusion | bytes 2359808 | tf_op jit(solution)/shard_map/jit(_take)/gather | solution.py:14
  354.5 1.9 select_bitcast_fusion.6
  356.3 1.4 copy.47
  357.8 1.4 copy.48
  359.2 1.9 select_bitcast_fusion.4
  361.1 1.4 copy.49
  362.5 1.4 copy.50
  363.8 1.9 select_bitcast_fusion.2
  365.7 1.4 copy.51
  367.1 1.4 copy.52
  368.5 1.9 select_bitcast_fusion
  370.4 1.4 copy.53
  371.8 1.4 copy.54
  373.2 6.8 %multiply_select_fusion = f32[9,256,128]{2,1,0:T(8,128)} fusion(f32[8,256,128]{2,1,0:T(8,128)} %fusion, f32[9,256,128]{2,1,0:T(8,128)S(1)} %multiply_select_fusion.1, f32[9,256,128]{2,1,0:T(8,128)} %bitcast.124, f32[9,256,128]{2,1,0:T(8,128)} %bitcast.123, f32[9,256,128]{2,1,0:T(8,128)} %bitcast.120, f32[9,256,128]{2,1,0:T(8,128)} %bitcast.118, ...), kind=kLoop, calls=%fused_computation.38 | loop fusion | flops 8257536 | bytes 12886656 | tf_op jit(solution)/shard_map/jit(_where)/select_n | solution.py:23
  (45 shorter events, 8.6 us)
Async XLA Ops:
  0.9 5.7 %copy-start.9 = (pred[512]{0:T(512)(128)(4,1)}, pred[512]{0:T(512)(128)(4,1)S(1)}, u32[]{:S(2)}) copy-start(pred[512]{0:T(512)(128)(4,1)S(1)} %compare_and_fusion.8) | copy-start | bytes 1540
  0.9 1.7 copy-start.6
  11.4 7.5 %copy-start.3 = (f32[8,9,128]{2,0,1:T(8,128)S(1)}, f32[8,9,128]{2,0,1:T(8,128)}, u32[]{:S(2)}) copy-start(f32[8,9,128]{2,0,1:T(8,128)} %param.12) | copy-start | bytes 110596
  11.4 12.3 %copy-start.11 = (s32[8,128]{1,0:T(8,128)S(1)}, s32[8,128]{1,0:T(8,128)}, u32[]{:S(2)}) copy-start(s32[8,128]{1,0:T(8,128)} %param.15) | copy-start | bytes 12292
  11.4 17.7 %copy-start.8 = (f32[9,128]{1,0:T(8,128)S(1)}, f32[9,128]{1,0:T(8,128)}, u32[]{:S(2)}) copy-start(f32[9,128]{1,0:T(8,128)} %param.14) | copy-start | bytes 13828
  11.4 18.3 %copy-start = (f32[9,256,128]{2,1,0:T(8,128)S(1)}, f32[9,256,128]{2,1,0:T(8,128)}, u32[]{:S(2)}) copy-start(f32[9,256,128]{2,1,0:T(8,128)} %param.11) | copy-start | bytes 3538948
  11.4 18.3 %copy-start.4 = (f32[8,128]{1,0:T(8,128)S(1)}, f32[8,128]{1,0:T(8,128)}, u32[]{:S(2)}) copy-start(f32[8,128]{1,0:T(8,128)} %param.13) | copy-start | bytes 12292
  11.4 112.7 %all-to-all-start = ((f32[2304,32,16]{0,2,1:T(8,128)}), f32[2304,32,16]{0,2,1:T(8,128)}, u32[]{:S(2)}, u32[]{:S(2)}) async-start(f32[2304,32,16]{0,2,1:T(8,128)} %bitcast.109), calls=%async_computation | async-start | bytes 9437184 | tf_op jit(solution)/shard_map/all_to_all | solution.py:38
  180.4 1.4 copy-start.2
  187.8 0.7 copy-start.7
  188.5 4.0 %copy-start.10 = (pred[512]{0:T(512)(128)(4,1)S(1)}, pred[512]{0:T(512)(128)(4,1)}, u32[]{:S(2)}) copy-start(pred[512]{0:T(512)(128)(4,1)} %copy-done.9) | copy-start | bytes 1540
  197.3 3.9 %copy-start.5 = (f32[8,128]{1,0:T(8,128)S(1)}, f32[8,128]{1,0:T(8,128)}, u32[]{:S(2)}) copy-start(f32[8,128]{1,0:T(8,128)} %param.13) | copy-start | bytes 12292
  197.3 109.2 %all-to-all-start.1 = ((f32[2304,32,16]{0,2,1:T(8,128)}), f32[2304,32,16]{0,2,1:T(8,128)}, u32[]{:S(2)}, u32[]{:S(2)}) async-start(f32[2304,32,16]{0,2,1:T(8,128)} %bitcast.110), calls=%async_computation.1 | async-start | bytes 9437184 | tf_op jit(solution)/shard_map/all_to_all | solution.py:38
  371.8 1.4 copy-start.1
where the time goes:
time: 381 us; the launch traced here: 380 us
  waiting for transfers between devices  198 us (52%)
  local copies, waits for them, and re-layouts  115 us (30%)
  other arithmetic  55.2 us (14%)
  starting transfers between devices  11.3 us (3%)
    all_to_all x2, waiting for transfers between devices, per_device(): lax.all_to_all(outgoing, 'cells', split_axis=1, concat_axis=1, tiled=True)  198 us
    gather x16, local copies, waits for them, and re-layouts, advance(): nearby = jnp.take(extended, columns, axis=1).reshape(levels, pulses, length)  77.6 us
    select_n x16, local copies, waits for them, and re-layouts, advance(): nearby = jnp.take(extended, columns, axis=1).reshape(levels, pulses, length)  22.6 us
    select_n x12, other arithmetic, advance(): nearby = jnp.take(extended, columns, axis=1).reshape(levels, pulses, length)  13.5 us
    select_n x2, other arithmetic, advance(): jnp.where(living[None, None, :], (values + summed + vertical) * (1.0 - de...  12.8 us
    all_to_all x2, starting transfers between devices, per_device(): lax.all_to_all(outgoing, 'cells', split_axis=1, concat_axis=1, tiled=True)  11.3 us
    concatenate x2, other arithmetic, per_device(): extended = jnp.concatenate([flat_values, incoming], axis=1)  10.5 us
    select_n x3, other arithmetic, per_device(): outgoing = jnp.take(flat_values, sender_rows.reshape(-1), axis=1)  9.7 us
  transfers between devices with their start and end apart: 2, of which 2 were waited for; matrix products, arithmetic and copies ran while one was open for 3% of the time, Pallas kernels for 0%

commit v1 on v0

--- a/solution.py
+++ b/solution.py
@@ -35,7 +35,12 @@
     for sweep in range(STEPS):
         flat_values = values.reshape(levels * pulses, capacity)
         outgoing = jnp.take(flat_values, sender_rows.reshape(-1), axis=1)
-        incoming = lax.all_to_all(outgoing, "cells", split_axis=1, concat_axis=1, tiled=True)
+        incoming = jnp.concatenate(
+            lax.all_to_all(
+                jnp.stack(jnp.split(outgoing, lax.axis_size("cells"), axis=1)), "cells", 0, 0
+            ),
+            axis=1,
+        )
         extended = jnp.concatenate([flat_values, incoming], axis=1)
         values = advance(
             values,

time: 381 us -> 421 us (1.10)
  local copies, waits for them, and re-layouts: 115 us -> 153 us
    unnamed x33 -> x81, local copies, waits for them, and re-layouts: 4.7 us -> 42.1 us
    select_n x3, other arithmetic: 9.7 us -> 5.42 us  [per_device(): outgoing = jnp.take(flat_values, sender_rows.reshape(-1), axis=1)]
    select_n x12 -> x16, other arithmetic: 13.5 us -> 17.2 us  [advance(): nearby = jnp.take(extended, columns, axis=1).reshape(levels, pulses, length)]
  transfers between devices with their start and end apart: 2 -> 2, of which waited for: 2 -> 2; matrix products, arithmetic and copies ran while one was open for 3% -> 2% of each run, Pallas kernels for 0% -> 0%
where the time goes in v1:
time: 421 us; the launch traced here: 419 us
  waiting for transfers between devices  202 us (48%)
  local copies, waits for them, and re-layouts  153 us (36%)
  other arithmetic  52.3 us (12%)
  starting transfers between devices  11.5 us (3%)
    all_to_all x2, waiting for transfers between devices, per_device(): lax.all_to_all(jnp.stack(jnp.split(outgoing, lax.axis_size('cells'), axis...  202 us
    gather x16, local copies, waits for them, and re-layouts, advance(): nearby = jnp.take(extended, columns, axis=1).reshape(levels, pulses, length)  76.6 us
    unnamed x81, local copies, waits for them, and re-layouts  42.1 us
    select_n x16, local copies, waits for them, and re-layouts, advance(): nearby = jnp.take(extended, columns, axis=1).reshape(levels, pulses, length)  20.5 us
    select_n x16, other arithmetic, advance(): nearby = jnp.take(extended, columns, axis=1).reshape(levels, pulses, length)  17.2 us
    select_n x2, other arithmetic, advance(): jnp.where(living[None, None, :], (values + summed + vertical) * (1.0 - de...  12.9 us
    all_to_all x2, starting transfers between devices, per_device(): lax.all_to_all(jnp.stack(jnp.split(outgoing, lax.axis_size('cells'), axis...  11.5 us
    concatenate x2, other arithmetic, per_device(): extended = jnp.concatenate([flat_values, incoming], axis=1)  10.5 us
  transfers between devices with their start and end apart: 2, of which 2 were waited for; matrix products, arithmetic and copies ran while one was open for 2% of the time, Pallas kernels for 0%

profile of v1, /device:TPU:0, one launch (start us, length us, event | category | flops | bytes accessed | tf_op | source)
XLA Modules:
  0.0 419.1 jit_solution(17385320879828167086)
XLA Ops:
  0.0 0.8 copy.27
  0.9 1.6 copy.29
  2.5 4.0 gather_fusion
  6.6 2.7 select_bitcast_fusion.1
  10.0 0.7 fusion.63
  30.7 7.6 %all-to-all-start = ((f32[32,2304,16]{1,2,0:T(8,128)}), f32[32,2304,16]{1,2,0:T(8,128)}, u32[]{:S(2)}, u32[]{:S(2)}) async-start(f32[32,2304,16]{1,2,0:T(8,128)} %fusion.33), calls=%async_computation | async-start | bytes 9437184 | tf_op jit(solution)/shard_map/all_to_all | solution.py:39
  45.0 1.1 subtract_multiply_fusion
  46.0 97.4 %all-to-all-done = f32[32,2304,16]{1,2,0:T(8,128)} async-done(((f32[32,2304,16]{1,2,0:T(8,128)}), f32[32,2304,16]{1,2,0:T(8,128)}, u32[]{:S(2)}, u32[]{:S(2)}) %all-to-all-start) | async-done | bytes 4718624 | tf_op jit(solution)/shard_map/all_to_all | solution.py:39
  143.4 5.2 %pad_maximum_fusion = f32[2304,640]{0,1:T(8,128)} fusion(f32[2304,512]{0,1:T(8,128)} %bitcast.38, f32[2304,128]{0,1:T(8,128)S(1)} %copy.29), kind=kLoop, calls=%fused_computation.18 | loop fusion | flops 1474560 | bytes 11796480 | tf_op jit(solution)/shard_map/concatenate | solution.py:44
  148.6 4.4 %gather_fusion.1 = f32[128,2304]{1,0:T(8,128)S(1)} fusion(f32[2304,640]{0,1:T(8,128)} %pad_maximum_fusion, s32[1024]{0:T(1024)} %get-tuple-element.52), kind=kCustom, calls=%fused_computation.1.clone | custom fusion | bytes 2359808 | tf_op jit(solution)/shard_map/jit(_take)/gather | solution.py:14
  153.0 0.8 select_bitcast_fusion.17
  153.8 1.5 copy.30
  155.3 4.4 %gather_fusion.2 = f32[128,2304]{1,0:T(8,128)S(1)} fusion(f32[2304,640]{0,1:T(8,128)} %pad_maximum_fusion, s32[1024]{0:T(1024)} %get-tuple-element.51), kind=kCustom, calls=%fused_computation.3.clone | custom fusion | bytes 2359808 | tf_op jit(solution)/shard_map/jit(_take)/gather | solution.py:14
  159.6 0.8 select_bitcast_fusion.16
  160.4 1.4 copy.32
  161.8 4.4 %gather_fusion.3 = f32[128,2304]{1,0:T(8,128)S(1)} fusion(f32[2304,640]{0,1:T(8,128)} %pad_maximum_fusion, s32[1024]{0:T(1024)} %get-tuple-element.50), kind=kCustom, calls=%fused_computation.4.clone | custom fusion | bytes 2359808 | tf_op jit(solution)/shard_map/jit(_take)/gather | solution.py:14
  166.2 0.8 select_bitcast_fusion.15
  167.0 1.4 copy.34
  168.4 4.4 %gather_fusion.4 = f32[128,2304]{1,0:T(8,128)S(1)} fusion(f32[2304,640]{0,1:T(8,128)} %pad_maximum_fusion, s32[1024]{0:T(1024)} %get-tuple-element.49), kind=kCustom, calls=%fused_computation.5.clone | custom fusion | bytes 2359808 | tf_op jit(solution)/shard_map/jit(_take)/gather | solution.py:14
  172.8 0.8 select_bitcast_fusion.14
  173.6 1.5 copy.36
  175.1 4.4 %gather_fusion.5 = f32[128,2304]{1,0:T(8,128)S(1)} fusion(f32[2304,640]{0,1:T(8,128)} %pad_maximum_fusion, s32[1024]{0:T(1024)} %get-tuple-element.48), kind=kCustom, calls=%fused_computation.6.clone | custom fusion | bytes 2359808 | tf_op jit(solution)/shard_map/jit(_take)/gather | solution.py:14
  179.4 0.8 select_bitcast_fusion.13
  180.3 1.4 copy.38
  181.7 4.4 %gather_fusion.6 = f32[128,2304]{1,0:T(8,128)S(1)} fusion(f32[2304,640]{0,1:T(8,128)} %pad_maximum_fusion, s32[1024]{0:T(1024)} %get-tuple-element.47), kind=kCustom, calls=%fused_computation.7.clone | custom fusion | bytes 2359808 | tf_op jit(solution)/shard_map/jit(_take)/gather | solution.py:14
  186.1 0.8 select_bitcast_fusion.12
  186.8 1.4 copy.40
  188.3 4.4 %gather_fusion.7 = f32[128,2304]{1,0:T(8,128)S(1)} fusion(f32[2304,640]{0,1:T(8,128)} %pad_maximum_fusion, s32[1024]{0:T(1024)} %get-tuple-element.46), kind=kCustom, calls=%fused_computation.8.clone | custom fusion | bytes 2359808 | tf_op jit(solution)/shard_map/jit(_take)/gather | solution.py:14
  192.6 0.8 select_bitcast_fusion.11
  193.5 1.4 copy.42
  194.8 4.4 %gather_fusion.8 = f32[128,2304]{1,0:T(8,128)S(1)} fusion(f32[2304,640]{0,1:T(8,128)} %pad_maximum_fusion, s32[1024]{0:T(1024)} %get-tuple-element.45), kind=kCustom, calls=%fused_computation.9.clone | custom fusion | bytes 2359808 | tf_op jit(solution)/shard_map/jit(_take)/gather | solution.py:14
  199.2 0.8 select_bitcast_fusion.10
  200.4 6.0 %multiply_select_fusion.1 = f32[9,256,128]{2,1,0:T(8,128)S(1)} fusion(f32[8,256,128]{2,1,0:T(8,128)} %subtract_multiply_fusion, f32[9,256,128]{2,1,0:T(8,128)S(1)} %copy-done, f32[9,256,128]{2,1,0:T(8,128)S(1)} %bitcast.375, f32[9,256,128]{2,1,0:T(8,128)} %bitcast.373, f32[9,256,128]{2,1,0:T(8,128)} %bitcast.371, f32[9,256,128]{2,1,0:T(8,128)} %bitcast.369, ...), kind=kLoop, calls=%fused_computation.39 | loop fusion | flops 8257536 | bytes 12886656 | tf_op jit(solution)/shard_map/jit(_where)/select_n | solution.py:23
  206.8 4.2 gather_fusion.9
  211.0 2.7 select_bitcast_fusion
  214.3 0.7 fusion.31
  235.0 3.9 all-to-all-start.1
  238.9 1.1 fusion
  240.0 104.2 %all-to-all-done.1 = f32[32,2304,16]{1,2,0:T(8,128)} async-done(((f32[32,2304,16]{1,2,0:T(8,128)}), f32[32,2304,16]{1,2,0:T(8,128)}, u32[]{:S(2)}, u32[]{:S(2)}) %all-to-all-start.1) | async-done | bytes 4718624 | tf_op jit(solution)/shard_map/all_to_all | solution.py:39
  344.2 5.2 %pad_maximum_fusion.1 = f32[2304,640]{0,1:T(8,128)} fusion(f32[2304,512]{0,1:T(8,128)} %bitcast.104, f32[2304,128]{0,1:T(8,128)S(1)} %copy.46), kind=kLoop, calls=%fused_computation.19 | loop fusion | flops 1474560 | bytes 11796480 | tf_op jit(solution)/shard_map/concatenate | solution.py:44
  349.5 5.4 %gather_fusion.10 = f32[128,2304]{1,0:T(8,128)} fusion(f32[2304,640]{0,1:T(8,128)} %pad_maximum_fusion.1, s32[1024]{0:T(1024)} %get-tuple-element.52), kind=kCustom, calls=%fused_computation.10.clone | custom fusion | bytes 2359808 | tf_op jit(solution)/shard_map/jit(_take)/gather | solution.py:14
  354.8 5.3 %gather_fusion.11 = f32[128,2304]{1,0:T(8,128)} fusion(f32[2304,640]{0,1:T(8,128)} %pad_maximum_fusion.1, s32[1024]{0:T(1024)} %get-tuple-element.51), kind=kCustom, calls=%fused_computation.11.clone | custom fusion | bytes 2359808 | tf_op jit(solution)/shard_map/jit(_take)/gather | solution.py:14
  360.2 5.3 %gather_fusion.12 = f32[128,2304]{1,0:T(8,128)} fusion(f32[2304,640]{0,1:T(8,128)} %pad_maximum_fusion.1, s32[1024]{0:T(1024)} %get-tuple-element.50), kind=kCustom, calls=%fused_computation.12.clone | custom fusion | bytes 2359808 | tf_op jit(solution)/shard_map/jit(_take)/gather | solution.py:14
  365.5 5.4 %gather_fusion.13 = f32[128,2304]{1,0:T(8,128)} fusion(f32[2304,640]{0,1:T(8,128)} %pad_maximum_fusion.1, s32[1024]{0:T(1024)} %get-tuple-element.49), kind=kCustom, calls=%fused_computation.13.clone | custom fusion | bytes 2359808 | tf_op jit(solution)/shard_map/jit(_take)/gather | solution.py:14
  370.9 5.4 %gather_fusion.14 = f32[128,2304]{1,0:T(8,128)} fusion(f32[2304,640]{0,1:T(8,128)} %pad_maximum_fusion.1, s32[1024]{0:T(1024)} %get-tuple-element.48), kind=kCustom, calls=%fused_computation.14.clone | custom fusion | bytes 2359808 | tf_op jit(solution)/shard_map/jit(_take)/gather | solution.py:14
  376.3 5.3 %gather_fusion.15 = f32[128,2304]{1,0:T(8,128)} fusion(f32[2304,640]{0,1:T(8,128)} %pad_maximum_fusion.1, s32[1024]{0:T(1024)} %get-tuple-element.47), kind=kCustom, calls=%fused_computation.15.clone | custom fusion | bytes 2359808 | tf_op jit(solution)/shard_map/jit(_take)/gather | solution.py:14
  381.6 5.3 %gather_fusion.16 = f32[128,2304]{1,0:T(8,128)} fusion(f32[2304,640]{0,1:T(8,128)} %pad_maximum_fusion.1, s32[1024]{0:T(1024)} %get-tuple-element.46), kind=kCustom, calls=%fused_computation.16.clone | custom fusion | bytes 2359808 | tf_op jit(solution)/shard_map/jit(_take)/gather | solution.py:14
  386.9 4.4 %gather_fusion.17 = f32[128,2304]{1,0:T(8,128)S(1)} fusion(f32[2304,640]{0,1:T(8,128)} %pad_maximum_fusion.1, s32[1024]{0:T(1024)} %get-tuple-element.45), kind=kCustom, calls=%fused_computation.17.clone | custom fusion | bytes 2359808 | tf_op jit(solution)/shard_map/jit(_take)/gather | solution.py:14
  391.3 1.4 select_bitcast_fusion.9
  392.7 1.4 copy.47
  394.1 1.4 select_bitcast_fusion.8
  395.5 1.4 copy.48
  396.9 1.4 select_bitcast_fusion.7
  398.4 1.4 copy.49
  399.8 1.4 select_bitcast_fusion.6
  401.2 1.4 copy.50
  402.6 1.4 select_bitcast_fusion.5
  404.0 1.4 copy.51
  405.4 1.4 select_bitcast_fusion.4
  406.8 1.4 copy.52
  408.2 1.4 select_bitcast_fusion.3
  409.7 1.4 copy.53
  411.0 0.8 select_bitcast_fusion.2
  412.2 6.8 %multiply_select_fusion = f32[9,256,128]{2,1,0:T(8,128)} fusion(f32[8,256,128]{2,1,0:T(8,128)} %fusion, f32[9,256,128]{2,1,0:T(8,128)S(1)} %multiply_select_fusion.1, f32[9,256,128]{2,1,0:T(8,128)S(1)} %bitcast.374, f32[9,256,128]{2,1,0:T(8,128)} %bitcast.372, f32[9,256,128]{2,1,0:T(8,128)} %bitcast.370, f32[9,256,128]{2,1,0:T(8,128)} %bitcast.368, ...), kind=kLoop, calls=%fused_computation.38 | loop fusion | flops 8257536 | bytes 12886656 | tf_op jit(solution)/shard_map/jit(_where)/select_n | solution.py:23
  (99 shorter events, 48.5 us)
Async XLA Ops:
  0.9 5.7 %copy-start.6 = (pred[512]{0:T(512)(128)(4,1)}, pred[512]{0:T(512)(128)(4,1)S(1)}, u32[]{:S(2)}) copy-start(pred[512]{0:T(512)(128)(4,1)S(1)} %compare_and_fusion.8) | copy-start | bytes 1540
  0.9 5.7 %copy-start.4 = (s32[1024]{0:T(1024)}, s32[1024]{0:T(1024)S(1)}, u32[]{:S(2)}) copy-start(s32[1024]{0:T(1024)S(1)} %pad_clamp_fusion.8) | copy-start | bytes 12292
  30.6 8.8 %copy-start.8 = (s32[8,128]{1,0:T(8,128)S(1)}, s32[8,128]{1,0:T(8,128)}, u32[]{:S(2)}) copy-start(s32[8,128]{1,0:T(8,128)} %param.15) | copy-start | bytes 12292
  30.6 11.9 %copy-start.5 = (f32[9,128]{1,0:T(8,128)S(1)}, f32[9,128]{1,0:T(8,128)}, u32[]{:S(2)}) copy-start(f32[9,128]{1,0:T(8,128)} %param.14) | copy-start | bytes 13828
  30.6 12.5 %copy-start.1 = (f32[8,9,128]{2,0,1:T(8,128)S(1)}, f32[8,9,128]{2,0,1:T(8,128)}, u32[]{:S(2)}) copy-start(f32[8,9,128]{2,0,1:T(8,128)} %param.12) | copy-start | bytes 110596
  30.6 14.3 %copy-start = (f32[9,256,128]{2,1,0:T(8,128)S(1)}, f32[9,256,128]{2,1,0:T(8,128)}, u32[]{:S(2)}) copy-start(f32[9,256,128]{2,1,0:T(8,128)} %param.11) | copy-start | bytes 3538948
  30.7 14.3 %copy-start.2 = (f32[8,128]{1,0:T(8,128)S(1)}, f32[8,128]{1,0:T(8,128)}, u32[]{:S(2)}) copy-start(f32[8,128]{1,0:T(8,128)} %param.13) | copy-start | bytes 12292
  30.7 112.7 %all-to-all-start = ((f32[32,2304,16]{1,2,0:T(8,128)}), f32[32,2304,16]{1,2,0:T(8,128)}, u32[]{:S(2)}, u32[]{:S(2)}) async-start(f32[32,2304,16]{1,2,0:T(8,128)} %fusion.33), calls=%async_computation | async-start | bytes 9437184 | tf_op jit(solution)/shard_map/all_to_all | solution.py:39
  206.8 4.2 copy-start.7
  235.0 3.9 copy-start.3
  235.0 109.2 %all-to-all-start.1 = ((f32[32,2304,16]{1,2,0:T(8,128)}), f32[32,2304,16]{1,2,0:T(8,128)}, u32[]{:S(2)}, u32[]{:S(2)}) async-start(f32[32,2304,16]{1,2,0:T(8,128)} %fusion.1), calls=%async_computation.1 | async-start | bytes 9437184 | tf_op jit(solution)/shard_map/all_to_all | solution.py:39
